TPU v7x, 128 devices: a whole 4x4x4 slice. The times are simulated.
128 devices in a mesh: pool: 4 (over x_hi, core), grp: 4 (over y), tp: 8 (over z, x_lo).
Axes of the slice: x: 4 (x_hi: 2, x_lo: 2; x = x_hi * 2 + x_lo), y: 4, z: 4, core: 2. Of those that a mesh axis runs over, the one named last changes fastest.
Arguments:
- hidden: bfloat16 [1024, 8192], P('pool', 'grp'), may hold values from -6 to 6
- attn_gain: float32 [8192], P('grp'), may hold values from 0.25 to 1.75
- w_query: bfloat16 [8192, 8192], P('grp', 'tp'), may hold values from -0.0625 to 0.0625
- w_key: bfloat16 [8192, 1024], P('grp', 'tp'), may hold values from -1 to 1
- w_value: bfloat16 [8192, 1024], P('grp', 'tp'), may hold values from -0.0625 to 0.0625
- w_out: bfloat16 [8192, 8192], P('tp', 'grp'), may hold values from -0.0625 to 0.0625
- prefix_keys: bfloat16 [8, 16384, 1024], P('pool', 'grp', 'tp'), may hold values from -300 to 300
- prefix_values: bfloat16 [8, 16384, 1024], P('pool', 'grp', 'tp'), may hold values from -6 to 6
- suffix_keys: bfloat16 [1024, 256, 1024], P('pool', 'grp', 'tp'), may hold values from -300 to 300
- suffix_values: bfloat16 [1024, 256, 1024], P('pool', 'grp', 'tp'), may hold values from -6 to 6
- prefix_ids: int32 [1024], P('pool'), may hold values from 0 to 7, as said below
- suffix_lens: int32 [1024], P('pool'), may hold values from 1 to 256, as said below
- ffn_gain: float32 [8192], P('grp'), may hold values from 0.25 to 1.75
- w_gate: bfloat16 [8192, 14336], P('grp', ('pool', 'tp')), may hold values from -0.0625 to 0.0625
- w_up: bfloat16 [8192, 14336], P('grp', ('pool', 'tp')), may hold values from -0.0625 to 0.0625
- w_down: bfloat16 [14336, 8192], P(('pool', 'tp'), 'grp'), may hold values from -0.046875 to 0.046875
Outputs:
- result: bfloat16 [1024, 8192], P(('pool', 'tp'), 'grp')
Inputs may be any that keep to these rules, and one draw needn't show every extreme that they name: `prefix_ids`: within rows p * 256 to (p + 1) * 256 - 1, each of the prefixes p * 2 to (p + 1) * 2 - 1 is named by exactly 128 streams, and no other prefix is named. `suffix_lens`: each block of 256 streams holds a stream of length 256 and one of length 1.
All inputs are finite; a program needn't handle non-finite values.
Results may differ from a plain program's by a relative error of at most 0.015.
Values may be sent and summed in bfloat16 or wider, within the bound.
No kernel may reach another device: no remote copies, remote signals or barrier semaphores. Data moves between devices by JAX's collectives and lax.ppermute only.
A program may use at most 192 MiB of HBM per device.

v0:
```python
import math
import jax
import jax.numpy as jnp
from jax import lax
from jax.sharding import PartitionSpec as P

D = 8192
HD = 128
epsilon = 1e-05


def joined(array, axis, combine):
    everything = jax.tree.map(lambda part: lax.all_gather(part, axis), array)
    first = jax.tree.map(lambda part: part[0], everything)

    def lap(k, so_far):
        return combine(so_far, jax.tree.map(lambda part: part[k], everything))

    return lax.fori_loop(1, lax.axis_size(axis), lap, first)


def combine_parts(earlier, later):
    peak_one, total_one, numer_one = earlier
    peak_two, total_two, numer_two = later
    peak = jnp.maximum(peak_one, peak_two)
    scale_one = jnp.exp(peak_one - peak)
    scale_two = jnp.exp(peak_two - peak)
    total = total_one * scale_one + total_two * scale_two
    numer = numer_one * scale_one[..., None] + numer_two * scale_two[..., None]
    return (peak, total, numer)


def body(
    hidden,
    attn_gain,
    w_query,
    w_key,
    w_value,
    w_out,
    prefix_keys,
    prefix_values,
    suffix_keys,
    suffix_values,
    prefix_ids,
    suffix_lens,
    ffn_gain,
    w_gate,
    w_up,
    w_down,
):
    stream_count = hidden.shape[0]
    hidden_float = hidden.astype(jnp.float32)
    squares = lax.psum(jnp.sum(hidden_float * hidden_float, axis=1), "grp")
    inverse = lax.rsqrt(squares / D + epsilon)
    normed = (hidden_float * inverse[:, None] * attn_gain).astype(jnp.bfloat16)
    part_query = jnp.dot(normed, w_query, preferred_element_type=jnp.float32)
    part_key = jnp.dot(normed, w_key, preferred_element_type=jnp.float32)
    part_value = jnp.dot(normed, w_value, preferred_element_type=jnp.float32)
    query, key_new, value_new = lax.psum((part_query, part_key, part_value), "grp")
    query = query.astype(jnp.bfloat16)
    key_new = key_new.astype(jnp.bfloat16)
    value_new = value_new.astype(jnp.bfloat16)
    kv_local = w_key.shape[1] // HD
    q_local = w_query.shape[1] // HD
    groups = q_local // kv_local
    prefix_local = prefix_keys.shape[0]
    pre_length = prefix_keys.shape[1]
    suf_length = suffix_keys.shape[1]
    factor = 1.0 / math.sqrt(HD)
    heads = query.reshape(stream_count, kv_local, groups, HD)
    pre_key = prefix_keys.reshape(prefix_local, pre_length, kv_local, HD)
    pre_value = prefix_values.reshape(prefix_local, pre_length, kv_local, HD)
    suf_key = suffix_keys.reshape(stream_count, suf_length, kv_local, HD)
    suf_value = suffix_values.reshape(stream_count, suf_length, kv_local, HD)
    local_prefix = prefix_ids - lax.axis_index("pool") * prefix_local
    per_group = stream_count // prefix_local
    one_hot = (local_prefix[:, None] == jnp.arange(prefix_local, dtype=jnp.int32)[None, :]).astype(
        jnp.int32
    )
    rank_within = jnp.sum(jnp.cumsum(one_hot, axis=0) * one_hot, axis=1) - 1
    target = local_prefix * per_group + rank_within
    group_order = (
        jnp.zeros((stream_count,), jnp.int32)
        .at[target]
        .set(jnp.arange(stream_count, dtype=jnp.int32))
    )
    grouped = heads[group_order].reshape(prefix_local, per_group, kv_local, groups, HD)
    pre_scores = (
        jnp.einsum("pskgd,pjkd->pskgj", grouped, pre_key, preferred_element_type=jnp.float32)
        * factor
    )
    pre_peak = pre_scores.max(axis=4).reshape(stream_count, kv_local, groups)[target]
    positions = lax.axis_index("grp") * suf_length + jnp.arange(suf_length, dtype=jnp.int32)
    valid = (positions[None, :] < suffix_lens[:, None])[:, None, None, :]
    suf_scores = (
        jnp.einsum("skgd,sjkd->skgj", heads, suf_key, preferred_element_type=jnp.float32) * factor
    )
    suf_scores = jnp.where(valid, suf_scores, -1e30)
    peak = jnp.maximum(pre_peak, suf_scores.max(axis=3))
    peak_grouped = peak[group_order].reshape(prefix_local, per_group, kv_local, groups)
    pre_weights = jnp.exp(pre_scores - peak_grouped[..., None]).astype(jnp.bfloat16)
    pre_total = (
        pre_weights.astype(jnp.float32).sum(axis=4).reshape(stream_count, kv_local, groups)[target]
    )
    pre_numer = jnp.einsum(
        "pskgj,pjkd->pskgd", pre_weights, pre_value, preferred_element_type=jnp.float32
    )
    pre_numer = pre_numer.reshape(stream_count, kv_local, groups, HD)[target]
    suf_weights = jnp.where(valid, jnp.exp(suf_scores - peak[:, :, :, None]), 0.0).astype(
        jnp.bfloat16
    )
    total = pre_total + suf_weights.astype(jnp.float32).sum(axis=3)
    numer = pre_numer + jnp.einsum(
        "skgj,sjkd->skgd", suf_weights, suf_value, preferred_element_type=jnp.float32
    )
    peak, total, numer = joined((peak, total, numer), "grp", combine_parts)
    own_score = (
        jnp.einsum(
            "skgd,skd->skg",
            heads,
            key_new.reshape(stream_count, kv_local, HD),
            preferred_element_type=jnp.float32,
        )
        * factor
    )
    new_peak = jnp.maximum(peak, own_score)
    rescale = jnp.exp(peak - new_peak)
    own_weight = jnp.exp(own_score - new_peak).astype(jnp.bfloat16).astype(jnp.float32)
    total = total * rescale + own_weight
    own_value = value_new.reshape(stream_count, kv_local, 1, HD).astype(jnp.float32)
    numer = numer * rescale[..., None] + own_weight[..., None] * own_value
    attended = (numer / total[..., None]).reshape(stream_count, q_local * HD).astype(jnp.bfloat16)
    partial_out = jnp.dot(attended, w_out, preferred_element_type=jnp.float32)
    share = stream_count // lax.axis_size("tp")
    tp_start = lax.axis_index("tp") * share
    summed = lax.psum(partial_out, "tp")
    summed = lax.dynamic_slice_in_dim(summed, tp_start, share, 0)
    own_hidden = lax.dynamic_slice_in_dim(hidden_float, tp_start, share, 0)
    middle = (own_hidden + summed).astype(jnp.bfloat16)
    gathered = lax.all_gather(middle, ("pool", "tp"), axis=0, tiled=True)
    gathered_float = gathered.astype(jnp.float32)
    ffn_squares = lax.psum(jnp.sum(gathered_float * gathered_float, axis=1), "grp")
    ffn_inverse = lax.rsqrt(ffn_squares / D + epsilon)
    normed_ffn = (gathered_float * ffn_inverse[:, None] * ffn_gain).astype(jnp.bfloat16)
    part_gate = jnp.dot(normed_ffn, w_gate, preferred_element_type=jnp.float32)
    part_upward = jnp.dot(normed_ffn, w_up, preferred_element_type=jnp.float32)
    gate, upward = lax.psum((part_gate, part_upward), "grp")
    act = (jax.nn.silu(gate) * upward).astype(jnp.bfloat16)
    returned = lax.psum_scatter(
        jnp.dot(act, w_down, preferred_element_type=jnp.float32),
        ("pool", "tp"),
        scatter_dimension=0,
        tiled=True,
    )
    return (middle.astype(jnp.float32) + returned).astype(jnp.bfloat16)


def solution(mesh):
    return jax.shard_map(
        body,
        mesh=mesh,
        in_specs=(
            P("pool", "grp"),
            P("grp"),
            P("grp", "tp"),
            P("grp", "tp"),
            P("grp", "tp"),
            P("tp", "grp"),
            P("pool", "grp", "tp"),
            P("pool", "grp", "tp"),
            P("pool", "grp", "tp"),
            P("pool", "grp", "tp"),
            P("pool"),
            P("pool"),
            P("grp"),
            P("grp", ("pool", "tp")),
            P("grp", ("pool", "tp")),
            P(("pool", "tp"), "grp"),
        ),
        out_specs=P(("pool", "tp"), "grp"),
        check_vma=False,
    )
```

profile of v0, /device:TPU:1, one launch (start us, length us, event | category | flops | bytes accessed | tf_op | source)
XLA Modules:
  0.0 672.8 jit_solution(15598244335575411505)
XLA Ops:
  9.7 9.5 %psum.56 = f32[256]{0:T(256)S(1)} all-reduce(f32[256]{0:T(256)S(1)} %multiply_reduce_fusion), channel_id=1, replica_groups=mesh['pool'=4,'grp'=4,'tp'=8] {'grp'}, use_global_device_ids=true, to_apply=%region_1.0 | all-reduce | flops 256 | bytes 2048 | tf_op jit(solution)/shard_map/psum | solution.py:53
  19.2 4.9 fusion.46
  25.2 26.5 %all-reduce.9 = (bf16[256,1024]{1,0:T(8,128)(2,1)S(1)}, bf16[256,128]{1,0:T(8,128)(2,1)S(1)}, bf16[256,128]{1,0:T(8,128)(2,1)S(1)}) all-reduce(f32[256,1024]{1,0:T(8,128)} %fusion.46, f32[256,128]{1,0:T(8,128)S(1)} %fusion.45, f32[256,128]{1,0:T(8,128)S(1)} %fusion.44), channel_id=1, replica_groups=mesh['pool'=4,'grp'=4,'tp'=8] {'grp'}, use_global_device_ids=true, to_apply=%region_2.0 | all-reduce | flops 327680 | bytes 1966080 | tf_op jit(solution)/shard_map/psum | solution.py:59
  55.4 13.1 %bitcast_reduce_fusion = (f32[2,128,8]{1,2,0:T(8,128)S(1)}, f32[2,128,8,4096]{3,1,2,0:T(8,128)}) fusion(bf16[2,4096,128]{2,1,0:T(8,128)(2,1)S(1)} %copy-done, bf16[2,128,8,128]{3,2,1,0:T(8,128)(2,1)S(1)} %bitcast.165), kind=kOutput, calls=%fused_computation.17 | convolution fusion | flops 2164258816 | bytes 36184064 | tf_op jit(solution)/shard_map/pskgd,pjkd->pskgj/dot_general | solution.py:89
  69.5 4.5 fusion.47
  74.9 13.8 %fusion.17 = f32[2,128,1,8,128]{4,1,3,0,2:T(8,128)S(1)} fusion(bf16[2,4096,128]{2,1,0:T(8,128)(2,1)} %param.25, f32[2,128,8]{1,2,0:T(8,128)S(1)} %copy.48, f32[2,128,8,4096]{3,1,2,0:T(8,128)} %get-tuple-element.234), kind=kOutput, calls=%fused_computation.37 | convolution fusion | flops 2172649472 | bytes 36708352 | tf_op jit(solution)/shard_map/pskgj,pjkd->pskgd/dot_general | solution.py:105
  90.3 2.9 gather_fusion.4
  93.2 4.7 convolution_add_fusion
  98.0 10.4 %all-gather.1 = f32[1024,8]{1,0:T(8,128)S(1)} all-gather(f32[256,8]{1,0:T(8,128)S(1)} %max.43), channel_id=3, replica_groups=mesh['pool'=4,'grp'=4,'tp'=8] {'grp'}, dimensions={0}, use_global_device_ids=true | all-gather | bytes 40960 | tf_op jit(solution)/shard_map/all_gather | solution.py:13
  108.5 14.6 %convert_reduce_fusion = f32[2,128,8]{1,2,0:T(8,128)S(1)} fusion(f32[2,128,8]{1,2,0:T(8,128)S(1)} %copy.48, f32[2,128,8,4096]{3,1,2,0:T(8,128)} %get-tuple-element.234), kind=kLoop, calls=%fused_computation.20 | loop fusion | flops 41940992 | bytes 33570816 | tf_op jit(solution)/shard_map/reduce_sum | solution.py:103
  124.8 14.8 %all-gather.2 = f32[1024,8]{1,0:T(8,128)S(1)} all-gather(f32[256,8]{1,0:T(8,128)S(1)} %add.162), channel_id=4, replica_groups=mesh['pool'=4,'grp'=4,'tp'=8] {'grp'}, dimensions={0}, use_global_device_ids=true | all-gather | bytes 40960 | tf_op jit(solution)/shard_map/all_gather | solution.py:13
  140.5 16.9 %all-gather.8.cloned.1.call-done = f32[1024,8,128]{2,1,0:T(8,128)} async-done(((f32[256,8,128]{2,1,0:T(8,128)}), f32[1024,8,128]{2,1,0:T(8,128)}) %all-gather.8.cloned.1.call-update) | async-done | bytes 4194320 | tf_op jit(solution)/shard_map/all_gather | solution.py:13
  158.7 6.7 while.19
  159.0 1.9 fusion.65
  166.9 4.8 fusion.28
  173.4 103.1 %all-reduce.6.cloned.1.call-done = f32[256,2048]{1,0:T(8,128)} async-done(((f32[256,2048]{1,0:T(8,128)}), f32[256,2048]{1,0:T(8,128)}) %all-reduce.6.cloned.1.call-update) | async-done | bytes 2097168 | tf_op jit(solution)/shard_map/psum | solution.py:136
  278.2 85.9 %all-gather.6.cloned.1.call-done = bf16[1024,2048]{1,0:T(8,128)(2,1)} async-done(((bf16[32,2048]{1,0:T(8,128)(2,1)}), bf16[1024,2048]{1,0:T(8,128)(2,1)}) %all-gather.6.cloned.1.call-update) | async-done | bytes 4194320 | tf_op jit(solution)/shard_map/all_gather | solution.py:140
  364.2 3.1 fusion.9
  367.2 8.5 %psum.61 = f32[1024]{0:T(1024)S(1)} all-reduce(f32[1024]{0:T(1024)S(1)} %fusion.9), channel_id=1, replica_groups=mesh['pool'=4,'grp'=4,'tp'=8] {'grp'}, use_global_device_ids=true, to_apply=%region_17.18 | all-reduce | flops 1024 | bytes 8192 | tf_op jit(solution)/shard_map/psum | solution.py:142
  375.7 6.4 fusion.22
  382.1 3.5 fusion.24
  385.6 85.0 %all-reduce.8.cloned.1.call-done = (f32[1024,448]{0,1:T(8,128)}, f32[1024,448]{0,1:T(8,128)}) async-done(((f32[1024,448]{0,1:T(8,128)}, f32[1024,448]{0,1:T(8,128)}), (f32[1024,448]{0,1:T(8,128)}, f32[1024,448]{0,1:T(8,128)})) %all-reduce.8.cloned.1.call-update) | async-done | bytes 3670032 | tf_op jit(solution)/shard_map/psum | solution.py:147
  470.7 8.3 %fusion.26 = f32[1024,2048]{1,0:T(8,128)} fusion(bf16[448,2048]{1,0:T(8,128)(2,1)} %param.33, f32[1024,448]{0,1:T(8,128)} %get-tuple-element.224, f32[1024,448]{0,1:T(8,128)} %get-tuple-element.225), kind=kOutput, calls=%fused_computation.44 | convolution fusion | flops 1881800704 | bytes 13893632 | tf_op jit(solution)/shard_map/dot_general | solution.py:150
  478.9 185.7 %reduce-scatter.2.cloned.1.call-done = f32[32,2048]{1,0:T(8,128)} async-done(((f32[1024,2048]{1,0:T(8,128)}), f32[32,2048]{1,0:T(8,128)}) %reduce-scatter.2.cloned.1.call-update) | async-done | bytes 262160 | tf_op jit(solution)/shard_map/reduce_scatter | solution.py:149
  (104 shorter events, 26.2 us)
Async XLA Ops:
  6.5 48.9 %copy-start = (bf16[2,4096,128]{2,1,0:T(8,128)(2,1)S(1)}, bf16[2,4096,128]{2,1,0:T(8,128)(2,1)}, u32[]{:S(2)}) copy-start(bf16[2,4096,128]{2,1,0:T(8,128)(2,1)} %param.24) | copy-start | bytes 6291460
  6.5 150.9 %all-gather.8.cloned.1.call-start = ((), (), s32[]{:S(2)}) async-start(), calls=%async_computation.4 | async-start | bytes 5242880 | tf_op jit(solution)/shard_map/all_gather | solution.py:13
  8.1 16.1 %copy-start.2 = (bf16[256,2048]{1,0:T(8,128)(2,1)S(1)}, bf16[256,2048]{1,0:T(8,128)(2,1)}, u32[]{:S(2)}) copy-start(bf16[256,2048]{1,0:T(8,128)(2,1)} %param.18) | copy-start | bytes 3145732
  8.1 16.1 %copy-start.11 = (f32[2048]{0:T(1024)S(1)}, f32[2048]{0:T(1024)}, u32[]{:S(2)}) copy-start(f32[2048]{0:T(1024)} %param.19) | copy-start | bytes 24580
  19.2 4.9 copy-start.9
  19.2 5.4 copy-start.10
  24.1 28.8 %copy-start.6 = (s32[256]{0:T(256)S(1)}, s32[256]{0:T(256)}, u32[]{:S(2)}) copy-start(s32[256]{0:T(256)} %param.28) | copy-start | bytes 3076
  55.4 14.0 %copy-start.7 = (s32[256]{0:T(256)S(1)}, s32[256]{0:T(256)}, u32[]{:S(2)}) copy-start(s32[256]{0:T(256)} %param.29) | copy-start | bytes 3076
  98.0 178.5 %all-reduce.6.cloned.1.call-start = ((), (), s32[]{:S(2)}) async-start(), calls=%async_computation.1 | async-start | bytes 4194304 | tf_op jit(solution)/shard_map/psum | solution.py:136
  166.8 4.9 copy-start.3
  171.7 204.0 %copy-start.12 = (f32[2048]{0:T(1024)S(1)}, f32[2048]{0:T(1024)}, u32[]{:S(2)}) copy-start(f32[2048]{0:T(1024)} %param.30) | copy-start | bytes 24580
  171.7 192.4 %all-gather.6.cloned.1.call-start = ((), (), s32[]{:S(2)}) async-start(), calls=%async_computation.2 | async-start | bytes 4325376 | tf_op jit(solution)/shard_map/all_gather | solution.py:140
  278.2 192.5 %all-reduce.8.cloned.1.call-start = ((), (), s32[]{:S(2)}) async-start(), calls=%async_computation.5 | async-start | bytes 7340032 | tf_op jit(solution)/shard_map/psum | solution.py:147
  375.7 6.4 copy-start.4
  375.7 6.4 copy-start.8
  385.6 279.0 %reduce-scatter.2.cloned.1.call-start = ((), (), s32[]{:S(2)}) async-start(), calls=%async_computation.3 | async-start | bytes 8650752 | tf_op jit(solution)/shard_map/reduce_scatter | solution.py:149
  478.9 187.3 %copy-start.1 = (bf16[2,4096,128]{2,1,0:T(8,128)(2,1)S(1)}, bf16[2,4096,128]{2,1,0:T(8,128)(2,1)}, u32[]{:S(2)}) copy-start(bf16[2,4096,128]{2,1,0:T(8,128)(2,1)} %param.24) | copy-start | bytes 6291460
  478.9 185.7 %copy-start.5 = (bf16[32,2048]{1,0:T(8,128)(2,1)S(1)}, bf16[32,2048]{1,0:T(8,128)(2,1)}, u32[]{:S(2)}) copy-start(bf16[32,2048]{1,0:T(8,128)(2,1)} %add_convert_fusion.1) | copy-start | bytes 393220
Sparse Core Ops, SparseCore 0:
  98.1 59.2 all-gather.7
  171.8 104.5 all-reduce.5
  278.3 85.8 all-gather.5
  385.7 84.8 all-reduce.7
  479.1 185.5 reduce-scatter.1
where the time goes:
time: 673 us
  waiting for transfers between devices  477 us (71%)
  blocking collectives  69.7 us (10%)
  matrix products  65.4 us (10%)
  other arithmetic  34.3 us (5%)
  between operations  13.5 us (2%)
  local copies, waits for them, and re-layouts  12.8 us (2%)
    reduce_scatter x1, waiting for transfers between devices, body(): lax.psum_scatter(jnp.dot(act, w_down, preferred_element_type=jnp.float32)...  186 us
    psum x1, waiting for transfers between devices, body(): summed = lax.psum(partial_out, 'tp')  103 us
    all_gather x1, waiting for transfers between devices, body(): gathered = lax.all_gather(middle, ('pool', 'tp'), axis=0, tiled=True)  85.9 us
    psum x1, waiting for transfers between devices, body(): gate, upward = lax.psum((part_gate, part_upward), 'grp')  85 us
    psum x1, blocking collectives, body(): lax.psum((part_query, part_key, part_value), 'grp')  26.5 us
    all_gather x2, blocking collectives, joined(): everything = jax.tree.map(lambda part: lax.all_gather(part, axis), array)  25.2 us
    all_gather x1, waiting for transfers between devices, joined(): everything = jax.tree.map(lambda part: lax.all_gather(part, axis), array)  16.9 us
    reduce_sum x1, other arithmetic, body(): pre_weights.astype(jnp.float32).sum(axis=4)  14.6 us
  transfers between devices with their start and end apart: 5, of which 5 were waited for; matrix products, arithmetic and copies ran while one was open for 3% of the time, Pallas kernels for 0%

commit v1 on v0

--- a/solution.py
+++ b/solution.py
@@ -133,7 +133,7 @@
     partial_out = jnp.dot(attended, w_out, preferred_element_type=jnp.float32)
     share = stream_count // lax.axis_size("tp")
     tp_start = lax.axis_index("tp") * share
-    summed = lax.psum(partial_out, "tp")
+    summed = jnp.sum(lax.all_gather(partial_out, "tp"), axis=0)
     summed = lax.dynamic_slice_in_dim(summed, tp_start, share, 0)
     own_hidden = lax.dynamic_slice_in_dim(hidden_float, tp_start, share, 0)
     middle = (own_hidden + summed).astype(jnp.bfloat16)

time: 673 us -> 903 us (1.34)
  waiting for transfers between devices: 477 us -> 699 us
    all_gather x0 -> x1, waiting for transfers between devices: none -> 324 us  [body(): summed = jnp.sum(lax.all_gather(partial_out, 'tp'), axis=0)]
    psum x1 -> x0, waiting for transfers between devices: 103 us -> none  [body(): summed = lax.psum(partial_out, 'tp')]
  transfers between devices with their start and end apart: 5 -> 5, of which waited for: 5 -> 5; matrix products, arithmetic and copies ran while one was open for 3% -> 2% of each run, Pallas kernels for 0% -> 0%
where the time goes in v1:
time: 903 us; the launch traced here: 902 us
  waiting for transfers between devices  699 us (77%)
  blocking collectives  69.7 us (8%)
  matrix products  64.4 us (7%)
  other arithmetic  42 us (5%)
  between operations  13.5 us (1%)
  local copies, waits for them, and re-layouts  12.8 us (1%)
    all_gather x1, waiting for transfers between devices, body(): summed = jnp.sum(lax.all_gather(partial_out, 'tp'), axis=0)  324 us
    reduce_scatter x1, waiting for transfers between devices, body(): lax.psum_scatter(jnp.dot(act, w_down, preferred_element_type=jnp.float32)...  186 us
    all_gather x1, waiting for transfers between devices, body(): gathered = lax.all_gather(middle, ('pool', 'tp'), axis=0, tiled=True)  87.3 us
    psum x1, waiting for transfers between devices, body(): gate, upward = lax.psum((part_gate, part_upward), 'grp')  84.7 us
    psum x1, blocking collectives, body(): lax.psum((part_query, part_key, part_value), 'grp')  26.5 us
    all_gather x2, blocking collectives, joined(): everything = jax.tree.map(lambda part: lax.all_gather(part, axis), array)  25.2 us
  transfers between devices with their start and end apart: 5, of which 5 were waited for; matrix products, arithmetic and copies ran while one was open for 2% of the time, Pallas kernels for 0%

profile of v1, /device:TPU:1, one launch (start us, length us, event | category | flops | bytes accessed | tf_op | source)
XLA Modules:
  0.0 902.2 jit_solution(10086700921107988655)
XLA Ops:
  9.7 9.5 %psum.49 = f32[256]{0:T(256)S(1)} all-reduce(f32[256]{0:T(256)S(1)} %multiply_reduce_fusion), channel_id=1, replica_groups=mesh['pool'=4,'grp'=4,'tp'=8] {'grp'}, use_global_device_ids=true, to_apply=%region_1.0 | all-reduce | flops 256 | bytes 2048 | tf_op jit(solution)/shard_map/psum | solution.py:53
  19.2 4.9 fusion.46
  25.2 26.5 %all-reduce.6 = (bf16[256,1024]{1,0:T(8,128)(2,1)S(1)}, bf16[256,128]{1,0:T(8,128)(2,1)S(1)}, bf16[256,128]{1,0:T(8,128)(2,1)S(1)}) all-reduce(f32[256,1024]{1,0:T(8,128)} %fusion.46, f32[256,128]{1,0:T(8,128)S(1)} %fusion.45, f32[256,128]{1,0:T(8,128)S(1)} %fusion.44), channel_id=1, replica_groups=mesh['pool'=4,'grp'=4,'tp'=8] {'grp'}, use_global_device_ids=true, to_apply=%region_2.0 | all-reduce | flops 327680 | bytes 1966080 | tf_op jit(solution)/shard_map/psum | solution.py:59
  55.4 13.1 %bitcast_reduce_fusion = (f32[2,128,8]{1,2,0:T(8,128)S(1)}, f32[2,128,8,4096]{3,1,2,0:T(8,128)}) fusion(bf16[2,4096,128]{2,1,0:T(8,128)(2,1)S(1)} %copy-done, bf16[2,128,8,128]{3,2,1,0:T(8,128)(2,1)S(1)} %bitcast.167), kind=kOutput, calls=%fused_computation.17 | convolution fusion | flops 2164258816 | bytes 36184064 | tf_op jit(solution)/shard_map/pskgd,pjkd->pskgj/dot_general | solution.py:89
  69.5 4.5 fusion.47
  74.9 13.8 %fusion.17 = f32[2,128,1,8,128]{4,1,3,0,2:T(8,128)S(1)} fusion(bf16[2,4096,128]{2,1,0:T(8,128)(2,1)} %param.25, f32[2,128,8]{1,2,0:T(8,128)S(1)} %copy.48, f32[2,128,8,4096]{3,1,2,0:T(8,128)} %get-tuple-element.234), kind=kOutput, calls=%fused_computation.37 | convolution fusion | flops 2172649472 | bytes 36708352 | tf_op jit(solution)/shard_map/pskgj,pjkd->pskgd/dot_general | solution.py:105
  90.3 2.9 gather_fusion.4
  93.2 4.7 convolution_add_fusion
  98.0 10.4 %all-gather.2 = f32[1024,8]{1,0:T(8,128)S(1)} all-gather(f32[256,8]{1,0:T(8,128)S(1)} %max.43), channel_id=4, replica_groups=mesh['pool'=4,'grp'=4,'tp'=8] {'grp'}, dimensions={0}, use_global_device_ids=true | all-gather | bytes 40960 | tf_op jit(solution)/shard_map/all_gather | solution.py:13
  108.5 14.6 %convert_reduce_fusion = f32[2,128,8]{1,2,0:T(8,128)S(1)} fusion(f32[2,128,8]{1,2,0:T(8,128)S(1)} %copy.48, f32[2,128,8,4096]{3,1,2,0:T(8,128)} %get-tuple-element.234), kind=kLoop, calls=%fused_computation.20 | loop fusion | flops 41940992 | bytes 33570816 | tf_op jit(solution)/shard_map/reduce_sum | solution.py:103
  124.8 14.8 %all-gather.3 = f32[1024,8]{1,0:T(8,128)S(1)} all-gather(f32[256,8]{1,0:T(8,128)S(1)} %add.160), channel_id=5, replica_groups=mesh['pool'=4,'grp'=4,'tp'=8] {'grp'}, dimensions={0}, use_global_device_ids=true | all-gather | bytes 40960 | tf_op jit(solution)/shard_map/all_gather | solution.py:13
  140.5 16.9 %all-gather.10.cloned.1.call-done = f32[1024,8,128]{2,1,0:T(8,128)} async-done(((f32[256,8,128]{2,1,0:T(8,128)}), f32[1024,8,128]{2,1,0:T(8,128)}) %all-gather.10.cloned.1.call-update) | async-done | bytes 4194320 | tf_op jit(solution)/shard_map/all_gather | solution.py:13
  158.7 6.7 while.19
  166.9 4.9 fusion.28
  173.4 324.4 %all-gather.12.cloned.1.call-done = f32[2048,2048]{1,0:T(8,128)} async-done(((f32[256,2048]{1,0:T(8,128)}), f32[2048,2048]{1,0:T(8,128)}) %all-gather.12.cloned.1.call-update) | async-done | bytes 16777232 | tf_op jit(solution)/shard_map/all_gather | solution.py:136
  497.8 7.8 reduce_sum.61
  507.3 87.3 %all-gather.8.cloned.1.call-done = bf16[1024,2048]{1,0:T(8,128)(2,1)} async-done(((bf16[32,2048]{1,0:T(8,128)(2,1)}), bf16[1024,2048]{1,0:T(8,128)(2,1)}) %all-gather.8.cloned.1.call-update) | async-done | bytes 4194320 | tf_op jit(solution)/shard_map/all_gather | solution.py:140
  594.6 3.1 fusion.9
  597.7 8.5 psum.53
  606.2 5.8 fusion.22
  612.0 3.5 fusion.24
  615.8 84.7 %all-reduce.5.cloned.1.call-done = (f32[1024,448]{0,1:T(8,128)}, f32[1024,448]{0,1:T(8,128)}) async-done(((f32[1024,448]{0,1:T(8,128)}, f32[1024,448]{0,1:T(8,128)}), (f32[1024,448]{0,1:T(8,128)}, f32[1024,448]{0,1:T(8,128)})) %all-reduce.5.cloned.1.call-update) | async-done | bytes 3670032 | tf_op jit(solution)/shard_map/psum | solution.py:147
  700.6 7.7 fusion.26
  708.3 185.7 %reduce-scatter.2.cloned.1.call-done = f32[32,2048]{1,0:T(8,128)} async-done(((f32[1024,2048]{1,0:T(8,128)}), f32[32,2048]{1,0:T(8,128)}) %reduce-scatter.2.cloned.1.call-update) | async-done | bytes 262160 | tf_op jit(solution)/shard_map/reduce_scatter | solution.py:149
  (109 shorter events, 28.3 us)
Async XLA Ops:
  6.5 48.9 %copy-start = (bf16[2,4096,128]{2,1,0:T(8,128)(2,1)S(1)}, bf16[2,4096,128]{2,1,0:T(8,128)(2,1)}, u32[]{:S(2)}) copy-start(bf16[2,4096,128]{2,1,0:T(8,128)(2,1)} %param.24) | copy-start | bytes 6291460
  6.5 150.9 %all-gather.10.cloned.1.call-start = ((), (), s32[]{:S(2)}) async-start(), calls=%async_computation.3 | async-start | bytes 5242880 | tf_op jit(solution)/shard_map/all_gather | solution.py:13
  8.1 16.1 %copy-start.2 = (bf16[256,2048]{1,0:T(8,128)(2,1)S(1)}, bf16[256,2048]{1,0:T(8,128)(2,1)}, u32[]{:S(2)}) copy-start(bf16[256,2048]{1,0:T(8,128)(2,1)} %param.18) | copy-start | bytes 3145732
  8.1 16.1 %copy-start.13 = (f32[2048]{0:T(1024)S(1)}, f32[2048]{0:T(1024)}, u32[]{:S(2)}) copy-start(f32[2048]{0:T(1024)} %param.19) | copy-start | bytes 24580
  19.2 4.9 copy-start.11
  19.2 5.4 copy-start.12
  24.1 28.8 %copy-start.6 = (s32[256]{0:T(256)S(1)}, s32[256]{0:T(256)}, u32[]{:S(2)}) copy-start(s32[256]{0:T(256)} %param.28) | copy-start | bytes 3076
  55.4 14.0 %copy-start.7 = (s32[256]{0:T(256)S(1)}, s32[256]{0:T(256)}, u32[]{:S(2)}) copy-start(s32[256]{0:T(256)} %param.29) | copy-start | bytes 3076
  98.0 399.8 %all-gather.12.cloned.1.call-start = ((), (), s32[]{:S(2)}) async-start(), calls=%async_computation.4 | async-start | bytes 18874368 | tf_op jit(solution)/shard_map/all_gather | solution.py:136
  166.8 5.0 copy-start.3
  171.8 422.9 %all-gather.8.cloned.1.call-start = ((), (), s32[]{:S(2)}) async-start(), calls=%async_computation.1 | async-start | bytes 4325376 | tf_op jit(solution)/shard_map/all_gather | solution.py:140
  505.6 100.6 %copy-start.14 = (f32[2048]{0:T(1024)S(1)}, f32[2048]{0:T(1024)}, u32[]{:S(2)}) copy-start(f32[2048]{0:T(1024)} %param.30) | copy-start | bytes 24580
  507.2 98.9 %copy-start.8 = (bf16[2048,448]{0,1:T(8,128)(2,1)S(1)}, bf16[2048,448]{0,1:T(8,128)(2,1)}, u32[]{:S(2)}) copy-start(bf16[2048,448]{0,1:T(8,128)(2,1)} %param.32) | copy-start | bytes 5505028
  507.3 193.3 %all-reduce.5.cloned.1.call-start = ((), (), s32[]{:S(2)}) async-start(), calls=%async_computation.5 | async-start | bytes 7340032 | tf_op jit(solution)/shard_map/psum | solution.py:147
  606.2 5.8 copy-start.4
  606.2 5.8 copy-start.9
  612.0 88.6 %copy-start.10 = (bf16[448,2048]{1,0:T(8,128)(2,1)S(1)}, bf16[448,2048]{1,0:T(8,128)(2,1)}, u32[]{:S(2)}) copy-start(bf16[448,2048]{1,0:T(8,128)(2,1)} %param.33) | copy-start | bytes 5505028
  615.5 278.5 %reduce-scatter.2.cloned.1.call-start = ((), (), s32[]{:S(2)}) async-start(), calls=%async_computation.2 | async-start | bytes 8650752 | tf_op jit(solution)/shard_map/reduce_scatter | solution.py:149
  708.3 187.3 %copy-start.1 = (bf16[2,4096,128]{2,1,0:T(8,128)(2,1)S(1)}, bf16[2,4096,128]{2,1,0:T(8,128)(2,1)}, u32[]{:S(2)}) copy-start(bf16[2,4096,128]{2,1,0:T(8,128)(2,1)} %param.24) | copy-start | bytes 6291460
  708.3 185.7 %copy-start.5 = (bf16[32,2048]{1,0:T(8,128)(2,1)S(1)}, bf16[32,2048]{1,0:T(8,128)(2,1)}, u32[]{:S(2)}) copy-start(bf16[32,2048]{1,0:T(8,128)(2,1)} %add_convert_fusion.1) | copy-start | bytes 393220
Sparse Core Ops, SparseCore 0:
  98.1 59.2 all-gather.9
  171.9 325.8 all-gather.11
  507.4 87.2 all-gather.7
  615.6 84.8 all-reduce.4
  708.5 185.5 reduce-scatter.1
